TPU v7x, 32 devices: a whole 2x2x4 slice. The times are simulated.
32 devices in a mesh: kv: 4 (over x, core), blk: 8 (over z, y).
Axes of the slice: x: 2, y: 2, z: 4, core: 2. Of those that a mesh axis runs over, the one named last changes fastest.
Arguments:
- patches: bfloat16 [24, 256, 1408], P('blk'), may hold values from -6 to 6
- merged_grid: int32 [24, 2], P('blk'), may hold values from 1 to 8, as said below
- picture_start: int32 [24], P('blk'), may hold values from 0 to 4095, as said below
- vis_gain: float32 [1408], replicated, may hold values from 0.5 to 2
- vis_qkv: bfloat16 [1408, 3, 1408], P(None, None, 'kv'), may hold values from -2 to 2
- vis_out: bfloat16 [1408, 1408], P('kv'), may hold values from -0.15625 to 0.15625
- merge_weight: bfloat16 [1408, 4096], P(None, 'kv'), may hold values from -0.15625 to 0.15625
- text_embed: bfloat16 [4096, 4096], P('blk', 'kv'), may hold values from -6 to 6
- dec_gain: float32 [4096], replicated, may hold values from 0.1 to 1.9
- w_query: bfloat16 [4096, 2048], P(None, 'kv'), may hold values from -2 to 2
- w_keyval: bfloat16 [4096, 2, 1024], P(None, None, 'kv'), may hold values from -2 to 2
- w_out: bfloat16 [2048, 4096], P('kv'), may hold values from -0.5 to 0.5
- req_lengths: int32 [8], replicated, may hold values from 1 to 2048, as said below
- final_gain: float32 [4096], P('kv'), may hold values from 0.1 to 1.9
- table: bfloat16 [8192, 4096], P('blk', 'kv'), may hold values from -0.25 to 0.25
Outputs:
- hidden: bfloat16 [4096, 4096], P('blk', 'kv')
- last_norm: bfloat16 [8, 4096], P(None, 'kv')
- max_logit: float32 [8], replicated
Inputs may be any that keep to these rules, and one draw needn't show every extreme that they name: `merged_grid`: some picture has a grid of 8 x 8 merged cells. Picture p's merged rows go to consecutive positions from picture_start[p] on, all inside the block of 512 positions with block index p // 3; pictures never share a position. `req_lengths`: the first request ends inside positions 512 to 1023; the second request holds 2048 positions, more than any other.
All inputs are finite; a program needn't handle non-finite values.
Results may differ from a plain program's by a relative error of at most 0.017.
Values may be sent and summed in bfloat16 or wider, within the bound.
No kernel may reach another device: no remote copies, remote signals or barrier semaphores. Data moves between devices by JAX's collectives and lax.ppermute only.
A program may use at most 128 MiB of HBM per device.

v0:
```python
import math
import jax
import jax.numpy as jnp
from jax import lax
from jax.sharding import PartitionSpec as P

VHD = 88
D = 4096
QHEADS = 16
KVHEADS = 8
HD = 128


def layer_norm(inputs, gain):
    centre = jnp.mean(inputs, axis=-1, keepdims=True)
    centred = inputs - centre
    spread = jnp.mean(centred * centred, axis=-1, keepdims=True)
    return centred * lax.rsqrt(spread + 1e-06) * gain


def rotate(inputs, position):
    half_width = inputs.shape[-1] // 2
    inverse = 500000.0 ** (-jnp.arange(half_width, dtype=jnp.float32) * 2.0 / inputs.shape[-1])
    angles = position.astype(jnp.float32)[:, None] * inverse[None, :]
    cosine = jnp.cos(angles)[:, None, :]
    sine = jnp.sin(angles)[:, None, :]
    first = inputs[..., :half_width]
    second = inputs[..., half_width:]
    return jnp.concatenate(
        [first * cosine - second * sine, second * cosine + first * sine], axis=-1
    )


def request_info(row_index, req_lengths):
    ends_at = jnp.cumsum(req_lengths)
    starts_at = ends_at - req_lengths
    request_id = jnp.sum((row_index[:, None] >= ends_at[None, :]).astype(jnp.int32), axis=1)
    choose = request_id[:, None] == jnp.arange(req_lengths.shape[0], dtype=jnp.int32)[None, :]
    request_begin = jnp.sum(jnp.where(choose, starts_at[None, :], 0), axis=1)
    return (request_id, request_begin)


def on_device(
    patches,
    merged_grid,
    picture_start,
    vis_gain,
    vis_qkv,
    vis_out,
    merge_weight,
    text_embed,
    dec_gain,
    w_query,
    w_keyval,
    w_out,
    req_lengths,
    final_gain,
    table,
):
    pictures, patch_max, vis_width = patches.shape
    merged_max = patch_max // 4
    vis_cols = vis_qkv.shape[2]
    vis_heads = vis_cols // VHD
    tok_rows, feat_dev = text_embed.shape
    text_rows = lax.all_gather(text_embed, "kv", axis=1, tiled=True)
    inputs = patches.astype(jnp.float32)
    normed = layer_norm(inputs, vis_gain).astype(jnp.bfloat16)
    packed = jnp.einsum(
        "pnd,dce->pnce", normed, vis_qkv, preferred_element_type=jnp.float32
    ).astype(jnp.bfloat16)
    packed = packed.reshape(pictures, patch_max, 3, vis_heads, VHD)
    scores = jnp.einsum(
        "pqhd,pkhd->phqk", packed[:, :, 0], packed[:, :, 1], preferred_element_type=jnp.float32
    ) / math.sqrt(VHD)
    cell_count = merged_grid[:, 0] * merged_grid[:, 1]
    valid_cols = jnp.arange(patch_max, dtype=jnp.int32)[None, :] < 4 * cell_count[:, None]
    scores = jnp.where(valid_cols[:, None, None, :], scores, -1e30)
    weights = jnp.exp(scores - jnp.max(scores, axis=-1, keepdims=True))
    weight_sum = jnp.sum(weights, axis=-1)
    mixed_rows = jnp.einsum(
        "phqk,pkhd->pqhd",
        weights.astype(jnp.bfloat16),
        packed[:, :, 2],
        preferred_element_type=jnp.float32,
    )
    mixed_rows = (
        (mixed_rows / jnp.transpose(weight_sum, (0, 2, 1))[..., None])
        .astype(jnp.bfloat16)
        .reshape(pictures, patch_max, vis_cols)
    )
    head_part = jnp.einsum("pnc,cd->pnd", mixed_rows, vis_out, preferred_element_type=jnp.float32)
    head_pooled = jnp.mean(head_part.reshape(pictures, merged_max, 4, vis_width), axis=2)
    head_total = lax.psum(head_pooled.astype(jnp.bfloat16), "kv").astype(jnp.float32)
    input_pooled = jnp.mean(inputs.reshape(pictures, merged_max, 4, vis_width), axis=2)
    pooled = (input_pooled + head_total).astype(jnp.bfloat16)
    merged = jnp.einsum(
        "pmd,de->pme", pooled, merge_weight, preferred_element_type=jnp.float32
    ).astype(jnp.bfloat16)
    block_base = lax.axis_index("blk") * tok_rows
    slot_index = jnp.arange(merged_max, dtype=jnp.int32)
    target = picture_start[:, None] + slot_index[None, :] - block_base
    target = jnp.where(slot_index[None, :] < cell_count[:, None], target, -1).reshape(-1)
    local_rows = jnp.arange(tok_rows, dtype=jnp.int32)
    one_hot = local_rows[:, None] == target[None, :]
    placed = jnp.dot(
        one_hot.astype(jnp.bfloat16),
        merged.reshape(pictures * merged_max, feat_dev),
        preferred_element_type=jnp.float32,
    )
    is_vision = jnp.any(one_hot, axis=1)
    seq_in = jnp.where(is_vision[:, None], placed.astype(jnp.bfloat16), text_embed)
    merged_rows = lax.all_gather(
        merged.reshape(pictures * merged_max, feat_dev), "kv", axis=1, tiled=True
    )
    placed_rows = jnp.dot(
        one_hot.astype(jnp.bfloat16), merged_rows, preferred_element_type=jnp.float32
    )
    full_rows = jnp.where(is_vision[:, None], placed_rows.astype(jnp.bfloat16), text_rows)
    full_float = full_rows.astype(jnp.float32)
    dec_normed = (
        full_float
        * lax.rsqrt(jnp.mean(full_float * full_float, axis=-1, keepdims=True) + 1e-05)
        * dec_gain
    ).astype(jnp.bfloat16)
    per_group = QHEADS // KVHEADS
    kv_heads = w_keyval.shape[2] // HD
    row_ids = block_base + local_rows
    request_id, request_begin = request_info(row_ids, req_lengths)
    position = row_ids - request_begin
    query_proj = jnp.dot(dec_normed, w_query, preferred_element_type=jnp.float32).reshape(
        tok_rows, kv_heads * per_group, HD
    )
    query_proj = (
        rotate(query_proj, position)
        .astype(jnp.bfloat16)
        .reshape(tok_rows, kv_heads * per_group * HD)
    )
    key_value = jnp.einsum("td,dce->tce", dec_normed, w_keyval, preferred_element_type=jnp.float32)
    key_rows = (
        rotate(key_value[:, 0].reshape(tok_rows, kv_heads, HD), position)
        .astype(jnp.bfloat16)
        .reshape(tok_rows, kv_heads * HD)
    )
    value_rows = key_value[:, 1].astype(jnp.bfloat16)
    query_req, query_begin = request_info(row_ids, req_lengths)
    root = math.sqrt(HD)
    reqs = req_lengths.shape[0]
    ends_at = jnp.cumsum(req_lengths)
    last_ids = ends_at - 1
    picker = (local_rows[None, :] == (last_ids - block_base)[:, None]).astype(jnp.bfloat16)
    query_last = jnp.dot(picker, query_proj, preferred_element_type=jnp.float32)
    seq_last = jnp.dot(picker, seq_in, preferred_element_type=jnp.float32)
    extras = jnp.concatenate([query_last, seq_last], axis=1).astype(jnp.bfloat16).reshape(-1)
    kv_width = key_rows.shape[1]
    ship_width = 2 * kv_width
    extra_rows = -(-extras.shape[0] // ship_width)
    extras = jnp.pad(extras, (0, extra_rows * ship_width - extras.shape[0]))
    shipped = jnp.concatenate([key_rows, value_rows], axis=1)
    shipped = jnp.concatenate([shipped, extras.reshape(extra_rows, ship_width)], axis=0)
    gathered = lax.all_gather(shipped, "blk", axis=0, tiled=False)
    blocks = gathered.shape[0]
    q_cols = query_proj.shape[1]
    extras_all = gathered[:, tok_rows:].reshape(blocks, -1)[:, : reqs * (q_cols + feat_dev)]
    extras_all = jnp.sum(extras_all.astype(jnp.float32).reshape(blocks, reqs, -1), axis=0)
    query_last = extras_all[:, :q_cols].astype(jnp.bfloat16)
    seq_last = extras_all[:, q_cols:]
    group_queries = [
        query_proj[:, g * per_group * HD : (g + 1) * per_group * HD].reshape(
            tok_rows, per_group, HD
        )
        for g in range(kv_heads)
    ]
    block_index = lax.axis_index("blk")
    first_begin = query_begin[0]

    def block_step(kb, state):
        key_first = kb * tok_rows
        needed = (kb <= block_index) & (key_first + tok_rows - 1 >= first_begin)

        def compute(state):
            piece = lax.dynamic_index_in_dim(gathered, kb, 0, keepdims=False)
            key_ids = key_first + local_rows
            key_req, unused = request_info(key_ids, req_lengths)
            allowed = (key_ids[None, :] <= row_ids[:, None]) & (
                key_req[None, :] == query_req[:, None]
            )
            allowed = allowed[:, None, :]
            new_state = []
            for g in range(kv_heads):
                run_max, run_sum, run_acc = state[g]
                keys_g = piece[:tok_rows, g * HD : (g + 1) * HD]
                values_g = piece[:tok_rows, kv_width + g * HD : kv_width + (g + 1) * HD]
                scores = (
                    jnp.einsum(
                        "tqd,kd->tqk", group_queries[g], keys_g, preferred_element_type=jnp.float32
                    )
                    / root
                )
                scores = jnp.where(allowed, scores, -1e30)
                new_max = jnp.maximum(run_max, jnp.max(scores, axis=-1))
                weights = jnp.where(allowed, jnp.exp(scores - new_max[..., None]), 0.0)
                scale = jnp.exp(run_max - new_max)
                new_sum = run_sum * scale + jnp.sum(weights, axis=-1)
                new_acc = run_acc * scale[..., None] + jnp.einsum(
                    "tqk,kd->tqd",
                    weights.astype(jnp.bfloat16),
                    values_g,
                    preferred_element_type=jnp.float32,
                )
                new_state.append((new_max, new_sum, new_acc))
            return tuple(new_state)

        return lax.cond(needed, compute, lambda s: s, state)

    init = tuple(
        (
            (
                jnp.full((tok_rows, per_group), -1e30, jnp.float32),
                jnp.zeros((tok_rows, per_group), jnp.float32),
                jnp.zeros((tok_rows, per_group, HD), jnp.float32),
            )
            for g in range(kv_heads)
        )
    )
    final = lax.fori_loop(0, blocks, block_step, init)
    context = jnp.concatenate(
        [
            (acc / total[..., None]).reshape(tok_rows, per_group * HD)
            for unused, total, acc in final
        ],
        axis=1,
    ).astype(jnp.bfloat16)
    all_ids = jnp.arange(blocks * tok_rows, dtype=jnp.int32)
    last_begin = ends_at - req_lengths
    last_allowed = (all_ids[None, :] >= last_begin[:, None]) & (
        all_ids[None, :] <= last_ids[:, None]
    )
    last_allowed = last_allowed[:, None, :]
    last_parts = []
    for g in range(kv_heads):
        keys_g = gathered[:, :tok_rows, g * HD : (g + 1) * HD].reshape(blocks * tok_rows, HD)
        values_g = gathered[:, :tok_rows, kv_width + g * HD : kv_width + (g + 1) * HD].reshape(
            blocks * tok_rows, HD
        )
        last_q = query_last[:, g * per_group * HD : (g + 1) * per_group * HD].reshape(
            reqs, per_group, HD
        )
        last_scores = (
            jnp.einsum("tqd,kd->tqk", last_q, keys_g, preferred_element_type=jnp.float32) / root
        )
        last_scores = jnp.where(last_allowed, last_scores, -1e30)
        last_max = jnp.max(last_scores, axis=-1)
        last_weights = jnp.where(last_allowed, jnp.exp(last_scores - last_max[..., None]), 0.0)
        last_sum = jnp.sum(last_weights, axis=-1)
        last_mix = jnp.einsum(
            "tqk,kd->tqd",
            last_weights.astype(jnp.bfloat16),
            values_g,
            preferred_element_type=jnp.float32,
        )
        last_parts.append((last_mix / last_sum[..., None]).reshape(reqs, per_group * HD))
    last_context = jnp.concatenate(last_parts, axis=1).astype(jnp.bfloat16)
    out_rows = jnp.concatenate([context, last_context], axis=0)
    head_sum = lax.psum_scatter(
        jnp.dot(out_rows, w_out, preferred_element_type=jnp.float32).astype(jnp.bfloat16),
        "kv",
        scatter_dimension=1,
        tiled=True,
    ).astype(jnp.float32)
    hidden = (seq_in.astype(jnp.float32) + head_sum[:tok_rows]).astype(jnp.bfloat16)
    chosen = (seq_last + head_sum[tok_rows:]).astype(jnp.bfloat16).astype(jnp.float32)
    square_part = jnp.sum(chosen * chosen, axis=-1)
    scaled = (chosen * final_gain).astype(jnp.bfloat16)
    logit_part = lax.dot_general(
        scaled, table, (((1,), (1,)), ((), ())), preferred_element_type=jnp.float32
    )
    logit_sum, square_sum = (
        lax.psum(logit_part.astype(jnp.bfloat16), "kv").astype(jnp.float32),
        lax.psum(square_part.astype(jnp.bfloat16), "kv").astype(jnp.float32),
    )
    inv_rms = lax.rsqrt(square_sum / D + 1e-05)
    last_norm = (chosen * inv_rms[:, None] * final_gain).astype(jnp.bfloat16)
    local_max = jnp.max(inv_rms[:, None] * logit_sum, axis=-1)
    max_logit = lax.pmax(local_max, "blk")
    return (hidden, last_norm, max_logit)


def solution(mesh):
    placed = (
        P("blk", None, None),
        P("blk", None),
        P("blk"),
        P(),
        P(None, None, "kv"),
        P("kv", None),
        P(None, "kv"),
        P("blk", "kv"),
        P(),
        P(None, "kv"),
        P(None, None, "kv"),
        P("kv", None),
        P(),
        P("kv"),
        P("blk", "kv"),
    )
    return jax.shard_map(
        on_device,
        mesh=mesh,
        in_specs=placed,
        out_specs=(P("blk", "kv"), P(None, "kv"), P()),
        check_vma=False,
    )
```

profile of v0, /device:TPU:0, one launch (start us, length us, event | category | flops | bytes accessed | tf_op | source)
XLA Modules:
  0.0 363.2 jit_solution(8306512292676467344)
XLA Ops:
  7.3 2.1 convert_reduce_fusion.1
  9.4 0.3 copy-done.2
  9.7 0.7 multiply_reduce_fusion
  10.5 2.9 fusion.58
  13.4 0.8 fusion.49
  14.2 0.7 fusion.50
  14.9 1.0 fusion.86
  15.9 0.6 copy.83
  16.6 0.7 dot_general.68
  17.3 1.3 convolution_reduce_fusion
  18.7 0.9 multiply_convert_fusion.1
  19.6 0.9 copy-done.3
  20.5 2.9 reshape.365
  23.4 4.8 %reduce_sum.145 = f32[3,64,1408]{2,1,0:T(8,128)S(1)} reduce(f32[3,64,4,1408]{3,2,1,0:T(4,128)} %reshape.365, f32[]{:T(128)} %constant.105.clone.1), dimensions={2}, to_apply=%region_1.0 | reduce | flops 811008 | bytes 5406724 | tf_op jit(solution)/shard_map/reduce_sum | solution.py:94
  28.2 27.3 %all-reduce.3.cloned.1.call-done = bf16[3,64,1408]{2,1,0:T(8,128)(2,1)} async-done(((bf16[3,64,1408]{2,1,0:T(8,128)(2,1)}), bf16[3,64,1408]{2,1,0:T(8,128)(2,1)}) %all-reduce.3.cloned.1.call-update) | async-done | bytes 540688 | tf_op jit(solution)/shard_map/psum | solution.py:93
  55.5 3.5 fusion.73
  59.1 0.7 all-gather.7.cloned.1.call-update
  59.8 0.2 all-gather.9.cloned.1.call-start
  60.2 0.2 reduce-window.15
  60.7 0.5 multiply_cosine_fusion
  61.3 1.6 fusion.72
  62.9 0.3 convolution_convert_fusion.4
  63.1 15.9 %all-gather.5.cloned.1.call-done = bf16[192,4096]{1,0:T(8,128)(2,1)} async-done(((bf16[192,1024]{1,0:T(8,128)(2,1)}), bf16[192,4096]{1,0:T(8,128)(2,1)}) %all-gather.5.cloned.1.call-update) | async-done | bytes 1572880 | tf_op jit(solution)/shard_map/all_gather | solution.py:112
  79.0 36.2 %all-gather.7.cloned.1.call-done = bf16[512,4096]{1,0:T(8,128)(2,1)} async-done(((bf16[512,1024]{1,0:T(8,128)(2,1)}), bf16[512,4096]{1,0:T(8,128)(2,1)}) %all-gather.7.cloned.1.call-update) | async-done | bytes 4194320 | tf_op jit(solution)/shard_map/all_gather | solution.py:65
  115.2 4.5 %fusion.30 = (f32[512]{0:T(512)S(1)}, bf16[512,4096]{1,0:T(8,128)(2,1)S(1)}) fusion(bf16[512,4096]{1,0:T(8,128)(2,1)} %all-gather.7.cloned.1.call-done, bf16[192,4096]{1,0:T(8,128)(2,1)} %all-gather.5.cloned.1.call-done, s32[192]{0:T(256)S(1)} %select_n.59, pred[512]{0:T(512)(128)(4,1)S(1)} %fusion.98), kind=kOutput, calls=%fused_computation.47 | convolution fusion | flops 815889920 | bytes 9964800 | tf_op jit(solution)/shard_map/dot_general | solution.py:115
  119.7 2.6 fusion.42
  122.4 2.6 fusion.76
  125.1 0.2 subtract_convert_fusion
  125.4 0.2 convolution_convert_fusion.5
  125.9 1.0 copy.87
  126.9 0.3 reduce-scatter.2.cloned.1.call-start
  127.2 0.5 slice.94
  127.9 0.2 copy.88
  128.0 0.2 copy.89
  128.2 74.7 %all-gather.9.cloned.1.call-done = bf16[4288,512]{1,0:T(8,128)(2,1)} async-done(((bf16[536,512]{1,0:T(8,128)(2,1)}), bf16[4288,512]{1,0:T(8,128)(2,1)}) %all-gather.9.cloned.1.call-update) | async-done | bytes 4390928 | tf_op jit(solution)/shard_map/all_gather | solution.py:160
  202.9 4.4 %fusion.120 = (bf16[8,512,128]{2,1,0:T(8,128)(2,1)}, bf16[8,512,128]{2,1,0:T(8,128)(2,1)}, bf16[8,512,128]{2,1,0:T(8,128)(2,1)}, bf16[8,512,128]{2,1,0:T(8,128)(2,1)}) fusion(bf16[8,536,512]{2,1,0:T(8,128)(2,1)} %bitcast.156), kind=kLoop, calls=%fused_computation.185 | loop fusion | bytes 8388608 | tf_op jit(solution)/shard_map/slice | solution.py:241
  207.3 1.0 convert_reduce_fusion.2
  208.2 0.8 broadcast.241
  209.1 0.8 broadcast.241.clone
  209.9 14.9 %while.28 = (s32[]{:T(128)}, f32[512,2]{0,1:T(2,128)S(1)}, f32[512,2]{0,1:T(2,128)S(1)}, f32[512,2,128]{2,0,1:T(8,128)}, f32[512,2]{0,1:T(2,128)S(1)}, /*index=5...) while((s32[]{:T(128)}, f32[512,2]{0,1:T(2,128)S(1)}, ...), condition=%wide.region_21.22_spmd.clone, body=%wide.region_12.21_spmd.clone.sunk | while | flops 551830080 | bytes 20388432 | solution.py:225
  210.6 9.5 %conditional.3 = ((f32[512,2]{0,1:T(2,128)S(1)}, f32[512,2]{0,1:T(2,128)S(1)}, f32[512,2,128]{2,0,1:T(8,128)}, f32[512,2]{0,1:T(2,128)S(1)}, f32[512,2]{0,1:T(2,128)S(1)}, /*index=5*/f32[512,2,128]{2,0,1:T(8,128)})) conditional(s32[]{:T(128)} %convert_element_type.269, (f32[512,2]{0,1:T(2,128)S(1)}, f32[512,2]{0,1:T(2,128)S(1)}, ...), branch_computations={%region_13.13_spmd, %region_14.20_spmd} | conditional | flops 551830080 | bytes 20385994 | solution.py:213
  210.6 1.1 dynamic-slice_bitcast_fusion
  211.7 0.4 fusion.21
  212.2 0.2 reduce-window.13
  212.4 0.3 compare_and_fusion
  212.7 0.8 fusion.5
  213.5 1.1 fusion.9
  214.6 2.7 convolution_add_fusion
  217.3 2.7 convolution_add_fusion.1
  224.8 1.3 copy.90
  226.1 1.2 copy.91
  227.4 1.9 fusion.123
  229.4 1.8 fusion.122
  231.2 0.2 fusion.82
  231.4 0.2 fusion.81
  232.0 6.6 %convolution_convert_fusion = bf16[520,4096]{1,0:T(8,128)(2,1)} fusion(bf16[512,4096]{1,0:T(8,128)(2,1)} %param.30, bf16[8,512]{0,1:T(8,128)(2,1)S(1)} %copy.92, bf16[512,256]{0,1:T(8,128)(2,1)S(1)} %bitcast.170, bf16[512,256]{0,1:T(8,128)(2,1)S(1)} %bitcast.171), kind=kOutput, calls=%fused_computation.50 | convolution fusion | flops 2184765440 | bytes 8986624 | tf_op jit(solution)/shard_map/dot_general | solution.py:265
  238.7 80.9 %reduce-scatter.2.cloned.1.call-done = bf16[520,1024]{1,0:T(8,128)(2,1)} async-done(((bf16[520,4096]{1,0:T(8,128)(2,1)}), bf16[520,1024]{1,0:T(8,128)(2,1)}) %reduce-scatter.2.cloned.1.call-update) | async-done | bytes 1064976 | tf_op jit(solution)/shard_map/reduce_scatter | solution.py:264
  319.5 1.6 convert_element_type.169
  321.3 1.3 fusion.57
  322.6 0.4 copy-done.8
  323.0 0.6 convolution_convert_fusion.3
  323.6 10.3 %all-reduce = (bf16[8]{0:T(256)(128)(2,1)S(1)}, bf16[8,1024]{1,0:T(8,128)(2,1)S(1)}) all-reduce(bf16[8]{0:T(256)(128)(2,1)S(1)} %get-tuple-element.768, bf16[8,1024]{1,0:T(8,128)(2,1)S(1)} %convolution_convert_fusion.3), channel_id=1, replica_groups=mesh['kv'=4,'blk'=8] {'kv'}, use_global_device_ids=true, to_apply=%region_29.30 | all-reduce | flops 8200 | bytes 32800 | tf_op jit(solution)/shard_map/psum | solution.py:279
  333.9 0.8 multiply_reduce_fusion.1
  334.7 22.0 %pmax.7 = f32[8]{0:T(128)} all-reduce(f32[8]{0:T(128)S(1)} %get-tuple-element.787), channel_id=1, replica_groups=mesh['kv'=4,'blk'=8] {'blk'}, use_global_device_ids=true, to_apply=%region_32.33 | all-reduce | flops 8 | bytes 64 | tf_op jit(solution)/shard_map/pmax | solution.py:284
  (101 shorter events, 2.2 us)
Async XLA Ops:
  7.2 3.3 copy-start
  7.2 3.2 copy-start.11
  7.2 3.3 copy-start.18
  7.2 48.3 %all-reduce.3.cloned.1.call-start = ((), (), s32[]{:S(2)}) async-start(), calls=%async_computation.1 | async-start | bytes 1081344 | tf_op jit(solution)/shard_map/psum | solution.py:93
  7.2 2.4 copy-start.2
  15.9 1.4 copy-start.16
  18.7 1.8 copy-start.3
  19.6 59.5 %all-gather.5.cloned.1.call-start = ((), (), s32[]{:S(2)}) async-start(), calls=%async_computation.2 | async-start | bytes 1966080 | tf_op jit(solution)/shard_map/all_gather | solution.py:112
  28.2 31.9 %copy-start.12 = (s32[3]{0:T(128)S(1)}, s32[3]{0:T(128)}, u32[]{:S(2)}) copy-start(s32[3]{0:T(128)} %param.21) | copy-start | bytes 40
  28.2 32.0 %copy-start.13 = (s32[8]{0:T(128)S(1)}, s32[8]{0:T(128)}, u32[]{:S(2)}) copy-start(s32[8]{0:T(128)} %param.31) | copy-start | bytes 100
  28.2 33.1 %copy-start.9 = (bf16[512,1024]{1,0:T(8,128)(2,1)S(1)}, bf16[512,1024]{1,0:T(8,128)(2,1)}, u32[]{:S(2)}) copy-start(bf16[512,1024]{1,0:T(8,128)(2,1)} %param.26) | copy-start | bytes 3145732
  59.1 56.1 %all-gather.7.cloned.1.call-start = ((), (), s32[]{:S(2)}) async-start(), calls=%async_computation.3 | async-start | bytes 5242880 | tf_op jit(solution)/shard_map/all_gather | solution.py:65
  59.8 143.1 %all-gather.9.cloned.1.call-start = ((), (), s32[]{:S(2)}) async-start(), calls=%async_computation.5 | async-start | bytes 4939776 | tf_op jit(solution)/shard_map/all_gather | solution.py:160
  62.8 56.8 %copy-start.4 = (bf16[512,1024]{1,0:T(8,128)(2,1)}, bf16[512,1024]{1,0:T(8,128)(2,1)S(1)}, u32[]{:S(2)}) copy-start(bf16[512,1024]{1,0:T(8,128)(2,1)S(1)} %fusion.72) | copy-start | bytes 3145732
  63.1 56.5 %copy-start.17 = (f32[4096]{0:T(1024)S(1)}, f32[4096]{0:T(1024)}, u32[]{:S(2)}) copy-start(f32[4096]{0:T(1024)} %param.27) | copy-start | bytes 49156
  115.2 4.5 %copy-start.14 = (bf16[4096,2,256]{2,1,0:T(2,128)(2,1)S(1)}, bf16[4096,2,256]{2,1,0:T(2,128)(2,1)}, u32[]{:S(2)}) copy-start(bf16[4096,2,256]{2,1,0:T(2,128)(2,1)} %param.29) | copy-start | bytes 12582916
  119.7 2.7 copy-start.15
  126.9 192.6 %reduce-scatter.2.cloned.1.call-start = ((), (), s32[]{:S(2)}) async-start(), calls=%async_computation.4 | async-start | bytes 5324800 | tf_op jit(solution)/shard_map/reduce_scatter | solution.py:264
  224.8 6.4 %copy-start.7 = (bf16[8,512,128]{2,1,0:T(8,128)(2,1)S(1)}, bf16[8,512,128]{2,1,0:T(8,128)(2,1)}, u32[]{:S(2)}) copy-start(bf16[8,512,128]{2,1,0:T(8,128)(2,1)} %get-tuple-element.776) | copy-start | bytes 3145732
  227.4 4.1 %copy-start.6 = (bf16[8,512,128]{2,1,0:T(8,128)(2,1)S(1)}, bf16[8,512,128]{2,1,0:T(8,128)(2,1)}, u32[]{:S(2)}) copy-start(bf16[8,512,128]{2,1,0:T(8,128)(2,1)} %get-tuple-element.774) | copy-start | bytes 3145732
  319.5 1.7 copy-start.5
  321.1 1.9 copy-start.8
  321.1 1.8 copy-start.10
  321.3 35.4 %copy-start.1 = (bf16[1408,3,352]{0,2,1:T(8,128)(2,1)S(1)}, bf16[1408,3,352]{0,2,1:T(8,128)(2,1)}, u32[]{:S(2)}) copy-start(bf16[1408,3,352]{0,2,1:T(8,128)(2,1)} %param.23) | copy-start | bytes 8921092
Sparse Core Ops, SparseCore 0:
  19.7 35.7 all-reduce.2
  59.2 19.7 all-gather.4
  80.7 34.4 all-gather.6
  127.0 75.8 all-gather.8
  238.8 80.7 reduce-scatter.1
where the time goes:
time: 364 us; the launch traced here: 363 us
  waiting for transfers between devices  236 us (65%)
  matrix products  39.4 us (11%)
  blocking collectives  32.2 us (9%)
  local copies, waits for them, and re-layouts  18 us (5%)
  other arithmetic  17.5 us (5%)
  between operations  14.3 us (4%)
  loops' own time  5.47 us (2%)
    reduce_scatter x1, waiting for transfers between devices, on_device(): lax.psum_scatter(jnp.dot(out_rows, w_out, preferred_element_type=jnp.floa...  80.9 us
    all_gather x1, waiting for transfers between devices, on_device(): gathered = lax.all_gather(shipped, 'blk', axis=0, tiled=False)  74.7 us
    all_gather x1, waiting for transfers between devices, on_device(): text_rows = lax.all_gather(text_embed, 'kv', axis=1, tiled=True)  36.2 us
    psum x1, waiting for transfers between devices, on_device(): lax.psum(head_pooled.astype(jnp.bfloat16), 'kv').astype(jnp.float32)  27.3 us
    pmax x1, blocking collectives, on_device(): max_logit = lax.pmax(local_max, 'blk')  22 us
    all_gather x1, waiting for transfers between devices, on_device(): lax.all_gather(merged.reshape(pictures * merged_max, feat_dev), 'kv', axi...  15.9 us
    psum x1, blocking collectives, on_device(): lax.psum(square_part.astype(jnp.bfloat16), 'kv').astype(jnp.float32)  10.3 us
  transfers between devices with their start and end apart: 5, of which 5 were waited for; matrix products, arithmetic and copies ran while one was open for 3% of the time, Pallas kernels for 0%

commit v1 on v0

--- a/solution.py
+++ b/solution.py
@@ -62,7 +62,12 @@
     vis_cols = vis_qkv.shape[2]
     vis_heads = vis_cols // VHD
     tok_rows, feat_dev = text_embed.shape
-    text_rows = lax.all_gather(text_embed, "kv", axis=1, tiled=True)
+    ring = [text_embed]
+    for hop in range(3):
+        ring.append(lax.ppermute(ring[-1], "kv", [(dev, (dev + 1) % 4) for dev in range(4)]))
+    text_rows = jnp.roll(
+        jnp.concatenate(ring[::-1], axis=1), (lax.axis_index("kv") + 1) * ring[0].shape[1], axis=1
+    )
     inputs = patches.astype(jnp.float32)
     normed = layer_norm(inputs, vis_gain).astype(jnp.bfloat16)
     packed = jnp.einsum(

time: 364 us -> 328 us (0.901)
  waiting for transfers between devices: 236 us -> 189 us
  local copies, waits for them, and re-layouts: 18 us -> 26.1 us
    all_gather x1 -> x0, waiting for transfers between devices: 36.2 us -> none  [on_device(): text_rows = lax.all_gather(text_embed, 'kv', axis=1, tiled=True)]
    ppermute x0 -> x3, waiting for transfers between devices: none -> 20.6 us  [on_device(): lax.ppermute(ring[-1], 'kv', [(dev, (dev + 1) % 4) for dev in range(4)])]
    all_gather x1, waiting for transfers between devices: 15.9 us -> 0.01 us  [on_device(): lax.all_gather(merged.reshape(pictures * merged_max, feat_dev), 'kv', axi...]
    reduce_scatter x1, waiting for transfers between devices: 80.9 us -> 66.9 us  [on_device(): lax.psum_scatter(jnp.dot(out_rows, w_out, preferred_element_type=jnp.floa...]
    unnamed x40 -> x39, local copies, waits for them, and re-layouts: 1.94 us -> 12.8 us
  transfers between devices with their start and end apart: 5 -> 7, of which waited for: 5 -> 5; matrix products, arithmetic and copies ran while one was open for 3% -> 13% of each run, Pallas kernels for 0% -> 0%
where the time goes in v1:
time: 328 us; the launch traced here: 327 us
  waiting for transfers between devices  189 us (58%)
  matrix products  37.2 us (11%)
  blocking collectives  32.2 us (10%)
  local copies, waits for them, and re-layouts  26.1 us (8%)
  other arithmetic  19.8 us (6%)
  between operations  14.3 us (4%)
  loops' own time  4.93 us (2%)
  starting transfers between devices  3.29 us (1%)
    all_gather x1, waiting for transfers between devices, on_device(): gathered = lax.all_gather(shipped, 'blk', axis=0, tiled=False)  74.9 us
    reduce_scatter x1, waiting for transfers between devices, on_device(): lax.psum_scatter(jnp.dot(out_rows, w_out, preferred_element_type=jnp.floa...  66.9 us
    psum x1, waiting for transfers between devices, on_device(): lax.psum(head_pooled.astype(jnp.bfloat16), 'kv').astype(jnp.float32)  26.7 us
    pmax x1, blocking collectives, on_device(): max_logit = lax.pmax(local_max, 'blk')  22 us
    ppermute x3, waiting for transfers between devices, on_device(): lax.ppermute(ring[-1], 'kv', [(dev, (dev + 1) % 4) for dev in range(4)])  20.6 us
    unnamed x39, local copies, waits for them, and re-layouts  12.8 us
    psum x1, blocking collectives, on_device(): lax.psum(square_part.astype(jnp.bfloat16), 'kv').astype(jnp.float32)  10.3 us
    dot_general x1, matrix products, on_device(): jnp.dot(out_rows, w_out, preferred_element_type=jnp.float32)  6.57 us
  transfers between devices with their start and end apart: 7, of which 5 were waited for; matrix products, arithmetic and copies ran while one was open for 13% of the time, Pallas kernels for 0%

profile of v1, /device:TPU:0, one launch (start us, length us, event | category | flops | bytes accessed | tf_op | source)
XLA Modules:
  0.0 327.0 jit_solution(11259035031260827775)
XLA Ops:
  7.2 0.5 collective-permute-start
  7.8 1.0 fusion.117
  8.8 2.0 convert_reduce_fusion.1
  10.8 0.7 multiply_reduce_fusion
  11.5 2.9 fusion.57
  14.4 0.8 fusion.48
  15.2 0.7 fusion.49
  16.0 1.0 fusion.85
  17.0 0.6 copy.83
  17.6 0.7 dot_general.68
  18.4 2.7 convolution_reduce_fusion
  21.1 0.9 multiply_convert_fusion.1
  22.3 0.2 collective-permute-done
  22.5 2.2 collective-permute-start.1
  24.7 2.9 reshape.365
  27.6 4.8 %reduce_sum.145 = f32[3,64,1408]{2,1,0:T(8,128)S(1)} reduce(f32[3,64,4,1408]{3,2,1,0:T(4,128)} %reshape.365, f32[]{:T(128)} %constant.128.clone.1), dimensions={2}, to_apply=%region_1.2 | reduce | flops 811008 | bytes 5406724 | tf_op jit(solution)/shard_map/reduce_sum | solution.py:99
  32.5 26.7 %all-reduce.3.cloned.1.call-done = bf16[3,64,1408]{2,1,0:T(8,128)(2,1)} async-done(((bf16[3,64,1408]{2,1,0:T(8,128)(2,1)}), bf16[3,64,1408]{2,1,0:T(8,128)(2,1)}) %all-reduce.3.cloned.1.call-update) | async-done | bytes 540688 | tf_op jit(solution)/shard_map/psum | solution.py:98
  59.3 3.5 %fusion.72 = bf16[3,64,1024]{2,1,0:T(8,128)(2,1)} fusion(bf16[1408,1024]{1,0:T(8,128)(2,1)} %param.25, bf16[3,64,1408]{2,1,0:T(8,128)(2,1)} %all-reduce.3.cloned.1.call-done, f32[3,64,1408]{2,1,0:T(8,128)S(1)} %reduce_sum.145), kind=kOutput, calls=%fused_computation.94 | convolution fusion | flops 554926080 | bytes 4898816 | tf_op jit(solution)/shard_map/pmd,de->pme/dot_general | solution.py:101
  63.2 0.2 collective-permute-start.2
  63.5 0.5 multiply_cosine_fusion
  64.0 1.6 fusion.71
  65.6 0.3 convolution_convert_fusion.4
  65.9 20.4 %collective-permute-done.2 = bf16[512,1024]{1,0:T(8,128)(2,1)S(1)} collective-permute-done((bf16[512,1024]{1,0:T(8,128)(2,1)}, bf16[512,1024]{1,0:T(8,128)(2,1)S(1)}, u32[]{:S(2)}, u32[]{:S(2)}) %collective-permute-start.2) | collective-permute-done | bytes 1048608 | tf_op jit(solution)/shard_map/ppermute | solution.py:67
  86.3 1.1 constant_dynamic-update-slice_fusion.7
  87.4 2.4 constant_dynamic-update-slice_fusion.6
  89.7 2.3 constant_dynamic-update-slice_fusion.5
  92.0 1.0 constant_dynamic-update-slice_fusion.4
  93.1 1.1 constant_dynamic-update-slice_fusion.3
  94.1 2.3 constant_dynamic-update-slice_fusion.2
  96.4 2.3 constant_dynamic-update-slice_fusion.1
  98.7 1.1 constant_dynamic-update-slice_fusion
  99.8 4.5 %fusion.30 = (f32[512]{0:T(512)S(1)}, bf16[512,4096]{1,0:T(8,128)(2,1)S(1)}) fusion(bf16[512,8192]{1,0:T(8,128)(2,1)} %constant_dynamic-update-slice_fusion, s32[]{:T(128)S(6)} %select_n.77, bf16[192,4096]{1,0:T(8,128)(2,1)} %all-gather.4.cloned.1.call-done, s32[192]{0:T(256)S(1)} %select_n.72, pred[512]{0:T(512)(128)(4,1)S(1)} %fusion.97), kind=kOutput, calls=%fused_computation.47 | convolution fusion | flops 815889920 | bytes 9964804 | tf_op jit(solution)/shard_map/dot_general | solution.py:120
  104.3 2.6 fusion.41
  107.0 2.6 fusion.75
  109.8 0.2 convolution_convert_fusion.5
  110.3 0.4 slice-done
  110.8 1.0 copy.87
  111.9 0.3 reduce-scatter.2.cloned.1.call-start
  112.2 0.5 slice.94
  113.1 74.9 %all-gather.6.cloned.1.call-done = bf16[4288,512]{1,0:T(8,128)(2,1)} async-done(((bf16[536,512]{1,0:T(8,128)(2,1)}), bf16[4288,512]{1,0:T(8,128)(2,1)}) %all-gather.6.cloned.1.call-update) | async-done | bytes 4390928 | tf_op jit(solution)/shard_map/all_gather | solution.py:165
  188.0 3.9 %fusion.119 = (bf16[8,512,128]{2,1,0:T(8,128)(2,1)}, bf16[8,512,128]{2,1,0:T(8,128)(2,1)S(1)}, bf16[8,512,128]{2,1,0:T(8,128)(2,1)}, bf16[8,512,128]{2,1,0:T(8,128)(2,1)S(1)}) fusion(bf16[8,536,512]{2,1,0:T(8,128)(2,1)} %bitcast.156), kind=kLoop, calls=%fused_computation.193 | loop fusion | bytes 8388608 | tf_op jit(solution)/shard_map/slice | solution.py:246
  192.0 1.0 convert_reduce_fusion.2
  193.0 1.8 fusion.121
  194.8 1.8 fusion.122
  196.6 0.2 fusion.80
  196.9 0.3 fusion.81
  197.4 10.8 %while.28 = (s32[]{:T(128)}, f32[512,2]{0,1:T(2,128)S(1)}, f32[512,2]{0,1:T(2,128)S(1)}, f32[512,2,128]{2,0,1:T(8,128)S(1)}, f32[512,2]{0,1:T(2,128)S(1)}, /*ind...) while((s32[]{:T(128)}, f32[512,2]{0,1:T(2,128)S(1)}, ...), condition=%wide.region_21.22_spmd.clone, body=%wide.region_12.21_spmd.clone.sunk | while | flops 551830080 | bytes 20388440 | solution.py:230
  198.0 5.9 %conditional.3 = ((f32[512,2]{0,1:T(2,128)S(1)}, f32[512,2]{0,1:T(2,128)S(1)}, f32[512,2,128]{2,0,1:T(8,128)S(1)}, f32[512,2]{0,1:T(2,128)S(1)}, f32[512,2]{0,1:T(2,128)S(1)}, /*index=5*/f32[512,2,128]{2,0,1:T(8,128)S(1)})) conditional(s32[]{:T(128)} %convert_element_type.269, (f32[512,2]{0,1:T(2,128)S(1)}, f32[512,2]{0,1:T(2,128)S(1)}, ...), branch_computations={%region_13.13_spmd, %region_14.20_spmd} | conditional | flops 551830080 | bytes 20385994 | solution.py:218
  198.3 0.3 compare_and_fusion
  198.6 1.1 dynamic-slice_bitcast_fusion
  199.7 0.4 fusion.21
  200.2 0.8 fusion.5
  201.0 1.0 fusion.9
  202.1 0.9 convolution_add_fusion.1
  203.0 0.9 convolution_add_fusion
  208.2 0.2 copy.91
  208.8 6.6 %convolution_convert_fusion = bf16[520,4096]{1,0:T(8,128)(2,1)} fusion(bf16[512,4096]{1,0:T(8,128)(2,1)} %param.30, bf16[8,512]{0,1:T(8,128)(2,1)S(1)} %copy.92, bf16[512,256]{0,1:T(8,128)(2,1)S(1)} %bitcast.170, bf16[512,256]{0,1:T(8,128)(2,1)S(1)} %bitcast.171), kind=kOutput, calls=%fused_computation.50 | convolution fusion | flops 2184765440 | bytes 8986624 | tf_op jit(solution)/shard_map/dot_general | solution.py:270
  215.4 66.9 %reduce-scatter.2.cloned.1.call-done = bf16[520,1024]{1,0:T(8,128)(2,1)} async-done(((bf16[520,4096]{1,0:T(8,128)(2,1)}), bf16[520,1024]{1,0:T(8,128)(2,1)}) %reduce-scatter.2.cloned.1.call-update) | async-done | bytes 1064976 | tf_op jit(solution)/shard_map/reduce_scatter | solution.py:269
  282.3 1.6 convert_element_type.169
  283.9 2.7 fusion.56
  286.8 0.6 convolution_convert_fusion.3
  287.5 10.3 %all-reduce = (bf16[8]{0:T(256)(128)(2,1)S(1)}, bf16[8,1024]{1,0:T(8,128)(2,1)S(1)}) all-reduce(bf16[8]{0:T(256)(128)(2,1)S(1)} %get-tuple-element.768, bf16[8,1024]{1,0:T(8,128)(2,1)S(1)} %convolution_convert_fusion.3), channel_id=1, replica_groups=mesh['kv'=4,'blk'=8] {'kv'}, use_global_device_ids=true, to_apply=%region_29.30 | all-reduce | flops 8200 | bytes 32800 | tf_op jit(solution)/shard_map/psum | solution.py:284
  297.7 0.8 multiply_reduce_fusion.1
  298.5 22.0 %pmax.7 = f32[8]{0:T(128)} all-reduce(f32[8]{0:T(128)S(1)} %get-tuple-element.787), channel_id=1, replica_groups=mesh['kv'=4,'blk'=8] {'blk'}, use_global_device_ids=true, to_apply=%region_32.33 | all-reduce | flops 8 | bytes 64 | tf_op jit(solution)/shard_map/pmax | solution.py:289
  (105 shorter events, 3.3 us)
Async XLA Ops:
  7.2 4.4 %copy-start = (bf16[1408,3,352]{0,2,1:T(8,128)(2,1)S(1)}, bf16[1408,3,352]{0,2,1:T(8,128)(2,1)}, u32[]{:S(2)}) copy-start(bf16[1408,3,352]{0,2,1:T(8,128)(2,1)} %param.23) | copy-start | bytes 8921092
  7.2 4.3 %copy-start.14 = (f32[1408]{0:T(1024)S(1)}, f32[1408]{0:T(1024)}, u32[]{:S(2)}) copy-start(f32[1408]{0:T(1024)} %param.22) | copy-start | bytes 16900
  7.2 52.1 %all-reduce.3.cloned.1.call-start = ((), (), s32[]{:S(2)}) async-start(), calls=%async_computation.1 | async-start | bytes 1081344 | tf_op jit(solution)/shard_map/psum | solution.py:98
  7.2 3.6 %copy-start.2 = (bf16[3,256,1408]{2,1,0:T(8,128)(2,1)S(1)}, bf16[3,256,1408]{2,1,0:T(8,128)(2,1)}, u32[]{:S(2)}) copy-start(bf16[3,256,1408]{2,1,0:T(8,128)(2,1)} %param.19) | copy-start | bytes 6488068
  7.2 15.2 %collective-permute-start = (bf16[512,1024]{1,0:T(8,128)(2,1)}, bf16[512,1024]{1,0:T(8,128)(2,1)}, u32[]{:S(2)}, u32[]{:S(2)}) collective-permute-start(bf16[512,1024]{1,0:T(8,128)(2,1)} %param.26), channel_id=1, source_target_pairs={{0,8},{8,16},{16,24},{24,0},{1,9},{9,17},{17,25},{25,1},{2,10},{10... | collective-permute-start | bytes 3145736 | tf_op jit(solution)/shard_map/ppermute | solution.py:67
  18.4 3.7 %copy-start.10 = (s32[8]{0:T(128)S(1)}, s32[8]{0:T(128)}, u32[]{:S(2)}) copy-start(s32[8]{0:T(128)} %param.31) | copy-start | bytes 100
  18.4 6.4 %copy-start.3 = (bf16[3,256,1408]{2,1,0:T(8,128)(2,1)S(1)}, bf16[3,256,1408]{2,1,0:T(8,128)(2,1)}, u32[]{:S(2)}) copy-start(bf16[3,256,1408]{2,1,0:T(8,128)(2,1)} %param.19) | copy-start | bytes 6488068
  22.0 77.7 %all-gather.4.cloned.1.call-start = ((), (), s32[]{:S(2)}) async-start(), calls=%async_computation.2 | async-start | bytes 1966080 | tf_op jit(solution)/shard_map/all_gather | solution.py:117
  22.5 40.7 %collective-permute-start.1 = (bf16[512,1024]{1,0:T(8,128)(2,1)}, bf16[512,1024]{1,0:T(8,128)(2,1)}, u32[]{:S(2)}, u32[]{:S(2)}) collective-permute-start(bf16[512,1024]{1,0:T(8,128)(2,1)} %collective-permute-done), channel_id=1, source_target_pairs={{0,8},{8,16},{16,24},{24,0},{1,9},{9,17},{17,25},{25,1},{2,10},{10... | collective-permute-start | bytes 3145736 | tf_op jit(solution)/shard_map/ppermute | solution.py:67
  27.6 4.8 %copy-start.9 = (s32[3]{0:T(128)S(1)}, s32[3]{0:T(128)}, u32[]{:S(2)}) copy-start(s32[3]{0:T(128)} %param.21) | copy-start | bytes 40
  32.4 31.6 %copy-start.4 = (bf16[512,1024]{1,0:T(8,128)(2,1)S(1)}, bf16[512,1024]{1,0:T(8,128)(2,1)}, u32[]{:S(2)}) copy-start(bf16[512,1024]{1,0:T(8,128)(2,1)} %param.26) | copy-start | bytes 3145732
  62.8 125.2 %all-gather.6.cloned.1.call-start = ((), (), s32[]{:S(2)}) async-start(), calls=%async_computation.4 | async-start | bytes 4939776 | tf_op jit(solution)/shard_map/all_gather | solution.py:165
  63.2 23.1 %collective-permute-start.2 = (bf16[512,1024]{1,0:T(8,128)(2,1)}, bf16[512,1024]{1,0:T(8,128)(2,1)S(1)}, u32[]{:S(2)}, u32[]{:S(2)}) collective-permute-start(bf16[512,1024]{1,0:T(8,128)(2,1)} %collective-permute-done.1), channel_id=1, source_target_pairs={{0,8},{8,16},{16,24},{24,0},{1,9},{9,17},{17,25},{25,1},{2,10},{10... | collective-permute-start | bytes 3145736 | tf_op jit(solution)/shard_map/ppermute | solution.py:67
  65.6 26.4 %copy-start.5 = (bf16[512,1024]{1,0:T(8,128)(2,1)}, bf16[512,1024]{1,0:T(8,128)(2,1)S(1)}, u32[]{:S(2)}) copy-start(bf16[512,1024]{1,0:T(8,128)(2,1)S(1)} %fusion.71) | copy-start | bytes 3145732
  99.8 4.5 %copy-start.13 = (f32[4096]{0:T(1024)S(1)}, f32[4096]{0:T(1024)}, u32[]{:S(2)}) copy-start(f32[4096]{0:T(1024)} %param.27) | copy-start | bytes 49156
  99.8 4.5 %copy-start.11 = (bf16[4096,2,256]{2,1,0:T(2,128)(2,1)S(1)}, bf16[4096,2,256]{2,1,0:T(2,128)(2,1)}, u32[]{:S(2)}) copy-start(bf16[4096,2,256]{2,1,0:T(2,128)(2,1)} %param.29) | copy-start | bytes 12582916
  104.3 2.7 copy-start.12
  106.9 2.7 copy-start.7
  109.6 1.0 slice-start
  111.9 170.4 %reduce-scatter.2.cloned.1.call-start = ((), (), s32[]{:S(2)}) async-start(), calls=%async_computation.3 | async-start | bytes 5324800 | tf_op jit(solution)/shard_map/reduce_scatter | solution.py:269
  215.4 71.4 %copy-start.8 = (f32[1024]{0:T(1024)S(1)}, f32[1024]{0:T(1024)}, u32[]{:S(2)}) copy-start(f32[1024]{0:T(1024)} %param.32) | copy-start | bytes 12292
  282.3 4.5 %copy-start.6 = (bf16[1024,1024]{1,0:T(8,128)(2,1)S(1)}, bf16[1024,1024]{1,0:T(8,128)(2,1)}, u32[]{:S(2)}) copy-start(bf16[1024,1024]{1,0:T(8,128)(2,1)} %param.33) | copy-start | bytes 6291460
  282.3 38.2 %copy-start.1 = (bf16[1408,3,352]{0,2,1:T(8,128)(2,1)S(1)}, bf16[1408,3,352]{0,2,1:T(8,128)(2,1)}, u32[]{:S(2)}) copy-start(bf16[1408,3,352]{0,2,1:T(8,128)(2,1)} %param.23) | copy-start | bytes 8921092
Sparse Core Ops, SparseCore 0:
  22.1 37.0 all-reduce.2
  62.9 24.0 all-gather.3
  112.0 75.9 all-gather.5
  215.5 66.7 reduce-scatter.1
